TPU v7x, 128 devices: a whole 4x4x4 slice. The times are simulated.
128 devices in a mesh: req: 8 (over y, x_hi), row: 4 (over x_lo, core), col: 4 (over z).
Axes of the slice: x: 4 (x_hi: 2, x_lo: 2; x = x_hi * 2 + x_lo), y: 4, z: 4, core: 2. Of those that a mesh axis runs over, the one named last changes fastest.
Arguments:
- text_embed: bfloat16 [6144, 4096], P(('req', 'col'), 'row')
- vis_embed: bfloat16 [4096, 4096], P(('req', 'col'), 'row')
- vis_segment: int32 [4096], P(('req', 'col')), may hold values from 0 to 20, never falling along the last dimension, each value on 1 to 256 neighbouring positions
- vis_valid: int32 [4096], P(('req', 'col')), may hold values 0 or 1
- vis_gain: bfloat16 [4096], P('row'), may hold values from 0.25 to 1.75
- vis_wq: bfloat16 [4096, 4096], P('row', 'col')
- vis_wk: bfloat16 [4096, 4096], P('row', 'col')
- vis_wv: bfloat16 [4096, 4096], P('row', 'col'), may hold values from -0.09375 to 0.09375
- vis_wo: bfloat16 [4096, 4096], P('col', 'row'), may hold values from -0.09375 to 0.09375
- dec_gain: bfloat16 [4096], P('row'), may hold values from 0.25 to 1.75
- dec_wq: bfloat16 [4096, 4096], P('row', 'col')
- dec_wk: bfloat16 [4096, 4096], P('row', 'col')
- dec_wv: bfloat16 [4096, 4096], P('row', 'col'), may hold values from -0.09375 to 0.09375
- dec_wo: bfloat16 [4096, 4096], P('col', 'row'), may hold values from -0.09375 to 0.09375
Outputs:
- hidden_out: bfloat16 [6144, 4096], P(('req', 'col'), 'row')
Inputs may be any that keep to these rules, and one draw needn't show every extreme that they name: `vis_segment`: images take consecutive slots in order, each 1 to 256 slots, one exactly 256.
All inputs are finite; a program needn't handle non-finite values. No bound on the sum of `vis_valid` on one device may be relied on, other than what follows from the above.
Results may differ from a plain program's by a relative error of at most 0.008.
Values may be sent and summed in bfloat16 or wider, within the bound.
No kernel may reach another device: no remote copies, remote signals or barrier semaphores. Data moves between devices by JAX's collectives and lax.ppermute only.
A program may use at most 192 MiB of HBM per device.

v0:
```python
import jax
import jax.numpy as jnp
from jax import lax
from jax.sharding import PartitionSpec as P

D = 4096
HD = 128
MAXIMG = 256


def with_halo(cells, sides, width):
    for axis, dim in sides:
        count = lax.axis_size(axis)
        ends = count - 1
        head = lax.slice_in_dim(cells, 0, width, axis=dim)
        tail = lax.slice_in_dim(cells, cells.shape[dim] - width, cells.shape[dim], axis=dim)
        cells = jnp.concatenate(
            [
                lax.ppermute(tail, axis, [(i, (i + 1) % count) for i in range(ends)]),
                cells,
                lax.ppermute(head, axis, [((i + 1) % count, i) for i in range(ends)]),
            ],
            axis=dim,
        )
    return cells


def passed_along(shard, axis, by):
    size = lax.axis_size(axis)
    pairs = [(i, i + by) for i in range(size) if 0 <= i + by < size]
    return lax.ppermute(shard, axis, pairs)


def norm_local(values, gain):
    floats = values.astype(jnp.float32)
    squares = jnp.sum(floats * floats, axis=-1)
    totals = lax.psum(squares, "row")
    factor = lax.rsqrt(totals / D + 1e-05)
    return (floats * factor[:, None] * gain.astype(jnp.float32)[None, :]).astype(jnp.bfloat16)


def gather_cols(values):
    return lax.all_gather(values, "col", axis=0, tiled=True)


def out_project(attended, weight):
    whole = lax.all_gather(attended, "row", axis=0, tiled=True)
    return lax.psum_scatter(
        jnp.dot(whole, weight, preferred_element_type=jnp.float32).astype(jnp.bfloat16),
        "col",
        scatter_dimension=0,
        tiled=True,
    ).astype(jnp.float32)


def split_heads(values):
    return values.reshape(values.shape[0], values.shape[1] // HD, HD)


def attend_block(queries, keys, values, allowed):
    query_heads = split_heads(queries)
    scores = jnp.einsum(
        "qhd,khd->hqk", query_heads, split_heads(keys), preferred_element_type=jnp.float32
    ) * HD ** (-0.5)
    scores = jnp.where(allowed[None], scores, -1e30)
    peak = jnp.max(scores, axis=-1, keepdims=True)
    weights = jnp.where(allowed[None], jnp.exp(scores - peak), 0.0)
    mass = jnp.sum(weights, axis=-1)
    summed = jnp.einsum(
        "hqk,khd->qhd",
        weights.astype(jnp.bfloat16),
        split_heads(values),
        preferred_element_type=jnp.float32,
    )
    result = summed / jnp.transpose(mass)[:, :, None]
    return result.reshape(queries.shape[0], queries.shape[1]).astype(jnp.bfloat16)


def fold_step(carry, query_heads, query_slots, key_heads, value_heads):
    peak, mass, accum = carry
    piece_slots = jnp.arange(key_heads.shape[0], dtype=jnp.int32)
    allowed = query_slots[:, None] >= piece_slots[None, :]
    scores = jnp.einsum(
        "qhd,khd->hqk", query_heads, key_heads, preferred_element_type=jnp.float32
    ) * HD ** (-0.5)
    scores = jnp.where(allowed[None], scores, -1e30)
    new_peak = jnp.maximum(peak, jnp.max(scores, axis=-1))
    weights = jnp.where(allowed[None], jnp.exp(scores - new_peak[:, :, None]), 0.0)
    summed = jnp.einsum(
        "hqk,khd->hqd",
        weights.astype(jnp.bfloat16),
        value_heads,
        preferred_element_type=jnp.float32,
    )
    return (new_peak, jnp.sum(weights, axis=-1), summed)


def start_state(head_count, query_count):
    return (
        jnp.full((head_count, query_count), -1e30, jnp.float32),
        jnp.zeros((head_count, query_count), jnp.float32),
        jnp.zeros((head_count, query_count, HD), jnp.float32),
    )


def head_project(values, weights):
    row_count = lax.axis_size("row")
    width = weights[0].shape[1]
    depth = weights[0].shape[0]
    shaped = jnp.stack(
        [w.reshape(depth, row_count, width // row_count) for w in weights], axis=2
    ).reshape(depth, row_count, len(weights) * (width // row_count))
    summed = jnp.einsum("tf,frc->rtc", values, shaped, preferred_element_type=jnp.float32)
    summed = summed.astype(jnp.bfloat16).reshape(row_count * values.shape[0], -1)
    return lax.psum_scatter(summed, "row", scatter_dimension=0, tiled=True)


def out_project_heads(attended, weight):
    row_count = lax.axis_size("row")
    whole = lax.all_gather(attended, "row", axis=0, tiled=False)
    shaped = weight.reshape(row_count, weight.shape[0] // row_count, weight.shape[1])
    summed = jnp.einsum("rtf,rfo->to", whole, shaped, preferred_element_type=jnp.float32)
    return lax.psum_scatter(
        summed.astype(jnp.bfloat16), "col", scatter_dimension=0, tiled=True
    ).astype(jnp.float32)


def per_device(
    text_embed,
    vis_embed,
    vis_segment,
    vis_valid,
    vis_gain,
    vis_wq,
    vis_wk,
    vis_wv,
    vis_wo,
    dec_gain,
    dec_wq,
    dec_wk,
    dec_wv,
    dec_wo,
):
    row_count = lax.axis_size("row")
    col_count = lax.axis_size("col")
    width = vis_wq.shape[1]
    local = width // row_count
    margin = MAXIMG - 1
    piece_ids = lax.all_gather(jnp.stack([vis_segment, vis_valid]), "col", axis=1, tiled=True)
    piece_len = piece_ids.shape[1]
    framed_ids = with_halo(piece_ids, (("req", 1),), margin)
    total_slots = piece_len * lax.axis_size("req")
    prompt_rows = text_embed.shape[0]
    prompt_total = prompt_rows * lax.axis_size("req") * col_count
    window_len = piece_len + 2 * margin
    window_start = lax.axis_index("req") * piece_len - margin
    window_index = jnp.arange(window_len, dtype=jnp.int32)
    key_slots = window_start + window_index
    inside = (key_slots >= 0) & (key_slots < total_slots)
    key_segment = framed_ids[0]
    key_valid = framed_ids[1]
    begins = jnp.concatenate([jnp.ones((1,), jnp.bool_), key_segment[1:] != key_segment[:-1]])
    begins = begins | (key_slots == 0)
    image_first = lax.cummax(jnp.where(begins, key_slots, window_start), axis=0)
    target_window = image_first * prompt_total // total_slots + key_slots - image_first
    vis_cols = gather_cols(norm_local(vis_embed, vis_gain))
    vis_proj = head_project(vis_cols, (vis_wq, vis_wk, vis_wv))
    vis_pairs = jnp.stack([vis_proj[:, local : 2 * local], vis_proj[:, 2 * local :]])
    framed = with_halo(vis_pairs, (("req", 1),), margin)
    query_local = margin + jnp.arange(piece_len, dtype=jnp.int32)
    query_slots = window_start + query_local
    query_segment = key_segment[query_local]
    seen = (
        inside[None, :]
        & (query_segment[:, None] == key_segment[None, :])
        & ((key_valid[None, :] == 1) | (query_slots[:, None] == key_slots[None, :]))
    )
    vis_att = attend_block(vis_proj[:, :local], framed[0], framed[1], seen)
    vis_out = (vis_embed.astype(jnp.float32) + out_project_heads(vis_att, vis_wo)).astype(
        jnp.bfloat16
    )
    device_place = lax.axis_index("req") * col_count + lax.axis_index("col")
    owned = device_place * prompt_rows + jnp.arange(prompt_rows, dtype=jnp.int32)
    slot_rows = vis_out.shape[0]
    following = passed_along(vis_out, ("req", "col"), -1)
    near_rows = jnp.concatenate([vis_out, following], axis=0)
    near_local = (
        margin + lax.axis_index("col") * slot_rows + jnp.arange(2 * slot_rows, dtype=jnp.int32)
    )
    near_slots = window_start + near_local
    present = near_slots < total_slots
    near_target = jnp.where(present, target_window[near_local], -1)
    near_valid = key_valid[near_local]
    onehot = ((owned[:, None] == near_target[None, :]) & (near_valid[None, :] == 1)).astype(
        jnp.bfloat16
    )
    carried = jnp.dot(onehot, near_rows, preferred_element_type=jnp.float32)
    mixed = (text_embed.astype(jnp.float32) + carried).astype(jnp.bfloat16)
    dec_cols = gather_cols(norm_local(mixed, dec_gain))
    dec_proj = head_project(dec_cols, (dec_wq, dec_wk, dec_wv))
    dec_rows = dec_cols.shape[0]
    dec_pairs = jnp.stack([dec_proj[:, local : 2 * local], dec_proj[:, 2 * local :]])
    piece = lax.all_gather(dec_pairs, "req", axis=1, tiled=True)
    token_slots = lax.axis_index("req") * dec_rows + jnp.arange(dec_rows, dtype=jnp.int32)
    all_slots = jnp.arange(piece.shape[1], dtype=jnp.int32)
    causal = token_slots[:, None] >= all_slots[None, :]
    dec_att = attend_block(dec_proj[:, :local], piece[0], piece[1], causal)
    return (mixed.astype(jnp.float32) + out_project_heads(dec_att, dec_wo)).astype(jnp.bfloat16)


def solution(mesh):
    return jax.shard_map(
        per_device,
        mesh=mesh,
        in_specs=(
            P(("req", "col"), "row"),
            P(("req", "col"), "row"),
            P(("req", "col")),
            P(("req", "col")),
            P("row"),
            P("row", "col"),
            P("row", "col"),
            P("row", "col"),
            P("col", "row"),
            P("row"),
            P("row", "col"),
            P("row", "col"),
            P("row", "col"),
            P("col", "row"),
        ),
        out_specs=P(("req", "col"), "row"),
        check_vma=False,
    )
```

profile of v0, /device:TPU:0, one launch (start us, length us, event | category | flops | bytes accessed | tf_op | source)
XLA Modules:
  0.0 511.5 jit_solution(722304668159904372)
XLA Ops:
  7.8 7.0 %psum.14 = f32[128]{0:T(128)S(1)} all-reduce(f32[128]{0:T(128)S(1)} %fusion.36), channel_id=1, replica_groups=mesh['req'=8,'row'=4,'col'=4] {'row'}, use_global_device_ids=true, to_apply=%region_3.4 | all-reduce | flops 128 | bytes 1024 | tf_op jit(solution)/shard_map/psum | solution.py:37
  25.2 4.0 copy.43
  29.2 6.6 %pad_maximum_fusion = bf16[1024,4,3,256]{0,3,2,1:T(8,128)(2,1)} fusion(bf16[1024,4,1,256]{0,3,2,1:T(8,128)(2,1)} %bitcast.89, bf16[1024,4,1,256]{0,3,2,1:T(8,128)(2,1)} %bitcast.88, bf16[1024,4,1,256]{0,3,2,1:T(8,128)(2,1)} %bitcast.87), kind=kLoop, calls=%fused_computation.14 | loop fusion | flops 6291456 | bytes 12582912 | tf_op jit(solution)/shard_map/stack | solution.py:110
  35.7 7.9 %all-gather.6.cloned.1.call-done = bf16[512,1024]{1,0:T(8,128)(2,1)} async-done(((bf16[128,1024]{1,0:T(8,128)(2,1)}), bf16[512,1024]{1,0:T(8,128)(2,1)}) %all-gather.6.cloned.1.call-update) | async-done | bytes 1048592 | tf_op jit(solution)/shard_map/all_gather | solution.py:43
  43.7 8.2 %convolution_convert_fusion.1 = bf16[4,768,512]{1,2,0:T(8,128)(2,1)} fusion(bf16[1024,4,768]{0,2,1:T(8,128)(2,1)} %bitcast.93, bf16[512,1024]{1,0:T(8,128)(2,1)} %all-gather.6.cloned.1.call-done), kind=kOutput, calls=%fused_computation.21 | convolution fusion | flops 3222798336 | bytes 10485760 | tf_op jit(solution)/shard_map/tf,frc->rtc/dot_general | solution.py:113
  51.9 4.7 copy.45
  57.2 8.6 %all_gather.20 = s32[2,512]{1,0:T(2,128)S(1)} all-gather(s32[2,128]{1,0:T(2,128)S(1)} %pad_add_fusion.1), channel_id=1, replica_groups=mesh['req'=8,'row'=4,'col'=4] {'col'}, dimensions={1}, use_global_device_ids=true | all-gather | bytes 5120 | tf_op jit(solution)/shard_map/all_gather | solution.py:149
  65.9 4.9 collective-permute-start
  72.1 5.6 %collective-permute-done.1 = s32[2,255]{1,0:T(2,128)S(1)} collective-permute-done((s32[2,255]{1,0:T(2,128)S(1)}, s32[2,255]{1,0:T(2,128)S(1)}, u32[]{:S(2)}, u32[]{:S(2)}) %collective-permute-start.1) | collective-permute-done | bytes 2072 | tf_op jit(solution)/shard_map/ppermute | solution.py:21
  77.8 16.1 %reduce-scatter.5.cloned.1.call-done = bf16[512,768]{0,1:T(8,128)(2,1)} async-done(((bf16[2048,768]{0,1:T(8,128)(2,1)}), bf16[512,768]{0,1:T(8,128)(2,1)}) %reduce-scatter.5.cloned.1.call-update) | async-done | bytes 786448 | tf_op jit(solution)/shard_map/reduce_scatter | solution.py:115
  96.0 5.3 %collective-permute-start.2 = (bf16[2,255,256]{1,2,0:T(8,128)(2,1)}, bf16[2,255,256]{1,2,0:T(8,128)(2,1)}, u32[]{:S(2)}, u32[]{:S(2)}) collective-permute-start(bf16[2,255,256]{1,2,0:T(8,128)(2,1)} %get-tuple-element.15), channel_id=1, source_target_pairs={{0,16},{16,32},{32,48},{48,64},{64,80},{80,96},{96,112},{1,17},{17... | collective-permute-start | bytes 783368 | tf_op jit(solution)/shard_map/ppermute | solution.py:19
  106.7 7.8 %collective-permute-done.3 = bf16[2,255,256]{1,2,0:T(8,128)(2,1)} collective-permute-done((bf16[2,255,256]{1,2,0:T(8,128)(2,1)}, bf16[2,255,256]{1,2,0:T(8,128)(2,1)}, u32[]{:S(2)}, u32[]{:S(2)}) %collective-permute-start.3) | collective-permute-done | bytes 261152 | tf_op jit(solution)/shard_map/ppermute | solution.py:21
  116.9 4.6 fusion.72
  124.9 21.4 %all-gather.8.cloned.1.call-done = bf16[4,512,256]{2,1,0:T(8,128)(2,1)} async-done(((bf16[1,512,256]{2,1,0:T(8,128)(2,1)}), bf16[4,512,256]{2,1,0:T(8,128)(2,1)}) %all-gather.8.cloned.1.call-update) | async-done | bytes 1048592 | tf_op jit(solution)/shard_map/all_gather | solution.py:120
  146.3 4.2 bitcast_convert_fusion.1
  152.8 22.6 %reduce-scatter.7.cloned.1.call-done = bf16[128,1024]{1,0:T(8,128)(2,1)} async-done(((bf16[512,1024]{1,0:T(8,128)(2,1)}), bf16[128,1024]{1,0:T(8,128)(2,1)}) %reduce-scatter.7.cloned.1.call-update) | async-done | bytes 262160 | tf_op jit(solution)/shard_map/reduce_scatter | solution.py:123
  179.3 5.4 %collective-permute-done.4 = bf16[128,1024]{1,0:T(8,128)(2,1)S(1)} collective-permute-done((bf16[128,1024]{1,0:T(8,128)(2,1)S(1)}, bf16[128,1024]{1,0:T(8,128)(2,1)S(1)}, u32[]{:S(2)}, u32[]{:S(2)}) %collective-permute-start.4) | collective-permute-done | bytes 262176 | tf_op jit(solution)/shard_map/ppermute | solution.py:31
  186.1 5.7 %psum.15 = f32[192]{0:T(256)S(1)} all-reduce(f32[192]{0:T(256)S(1)} %get-tuple-element.23), channel_id=1, replica_groups=mesh['req'=8,'row'=4,'col'=4] {'row'}, use_global_device_ids=true, to_apply=%region_9.10 | all-reduce | flops 192 | bytes 1536 | tf_op jit(solution)/shard_map/psum | solution.py:37
  204.5 6.6 %pad_maximum_fusion.1 = bf16[1024,4,3,256]{0,3,2,1:T(8,128)(2,1)} fusion(bf16[1024,4,1,256]{0,3,2,1:T(8,128)(2,1)} %bitcast.92, bf16[1024,4,1,256]{0,3,2,1:T(8,128)(2,1)} %bitcast.91, bf16[1024,4,1,256]{0,3,2,1:T(8,128)(2,1)} %bitcast.90), kind=kLoop, calls=%fused_computation.15 | loop fusion | flops 6291456 | bytes 12582912 | tf_op jit(solution)/shard_map/stack | solution.py:110
  211.2 12.1 %all-gather.10.cloned.1.call-done = bf16[768,1024]{1,0:T(8,128)(2,1)} async-done(((bf16[192,1024]{1,0:T(8,128)(2,1)}), bf16[768,1024]{1,0:T(8,128)(2,1)}) %all-gather.10.cloned.1.call-update) | async-done | bytes 1572880 | tf_op jit(solution)/shard_map/all_gather | solution.py:43
  223.3 9.1 %convolution_convert_fusion = bf16[4,768,768]{1,2,0:T(8,128)(2,1)} fusion(bf16[1024,4,768]{0,2,1:T(8,128)(2,1)} %bitcast.94, bf16[768,1024]{1,0:T(8,128)(2,1)} %all-gather.10.cloned.1.call-done), kind=kOutput, calls=%fused_computation.20 | convolution fusion | flops 4834197504 | bytes 12582912 | tf_op jit(solution)/shard_map/tf,frc->rtc/dot_general | solution.py:113
  232.4 6.6 %copy.53 = bf16[3072,768]{0,1:T(8,128)(2,1)} copy(bf16[3072,768]{1,0:T(8,128)(2,1)} %bitcast.95) | data formatting | bytes 9437184 | tf_op jit(solution)/shard_map/reshape | solution.py:114
  239.2 49.6 %reduce-scatter.9.cloned.1.call-done = bf16[768,768]{0,1:T(8,128)(2,1)} async-done(((bf16[3072,768]{0,1:T(8,128)(2,1)}), bf16[768,768]{0,1:T(8,128)(2,1)}) %reduce-scatter.9.cloned.1.call-update) | async-done | bytes 1179664 | tf_op jit(solution)/shard_map/reduce_scatter | solution.py:115
  291.1 5.7 %iota_compare_fusion = pred[768,6144]{1,0:T(8,128)(4,1)} fusion(s32[768]{0:T(1024)S(1)} %iota_add_fusion), kind=kLoop, calls=%fused_computation.12 | loop fusion | flops 4718592 | bytes 4721664 | tf_op jit(solution)/shard_map/ge | solution.py:206
  296.8 83.9 %all-gather.12.cloned.1.call-done = bf16[2,6144,256]{1,2,0:T(8,128)(2,1)} async-done(((bf16[2,768,256]{1,2,0:T(8,128)(2,1)}), bf16[2,6144,256]{1,2,0:T(8,128)(2,1)}) %all-gather.12.cloned.1.call-update) | async-done | bytes 6291472 | tf_op jit(solution)/shard_map/all_gather | solution.py:203
  380.7 5.4 %fusion.66 = (bf16[1,6144,256]{1,2,0:T(8,128)(2,1)S(1)}, bf16[1,6144,256]{1,2,0:T(8,128)(2,1)}) fusion(bf16[2,6144,256]{1,2,0:T(8,128)(2,1)} %all-gather.12.cloned.1.call-done), kind=kLoop, calls=%fused_computation.110 | loop fusion | bytes 12582912 | tf_op jit(solution)/shard_map/slice | solution.py:207
  386.1 14.7 %fusion.74 = f32[2,768,6144]{2,1,0:T(8,128)} fusion(bf16[768,2,128]{0,2,1:T(8,128)(2,1)S(1)} %bitcast.100, bf16[6144,2,128]{0,2,1:T(8,128)(2,1)S(1)} %bitcast.86), kind=kOutput, calls=%fused_computation.118 | convolution fusion | flops 2415919104 | bytes 41287680 | tf_op jit(solution)/shard_map/qhd,khd->hqk/dot_general | solution.py:62
  400.8 36.8 %fusion.73 = (f32[2,768]{1,0:T(2,128)S(1)}, bf16[2,768,6144]{2,1,0:T(8,128)(2,1)}) fusion(f32[2,768,6144]{2,1,0:T(8,128)} %fusion.74, pred[768,6144]{1,0:T(8,128)(4,1)S(1)} %bitcast.97), kind=kOutput, calls=%fused_computation.117 | output fusion | flops 75503616 | bytes 61347840 | tf_op jit(solution)/shard_map/sub | solution.py:67
  437.6 10.4 %fusion.32 = bf16[768,2,128]{0,2,1:T(8,128)(2,1)S(1)} fusion(bf16[6144,2,128]{0,2,1:T(8,128)(2,1)} %bitcast.99, bf16[2,768,6144]{2,1,0:T(8,128)(2,1)} %get-tuple-element.26, f32[768,2]{0,1:T(2,128)S(1)} %bitcast.111), kind=kOutput, calls=%fused_computation.38 | convolution fusion | flops 2416312320 | bytes 22419456 | tf_op jit(solution)/shard_map/hqk,khd->qhd/dot_general | solution.py:69
  449.0 22.7 %all-gather.14.cloned.1.call-done = bf16[4,768,256]{2,1,0:T(8,128)(2,1)} async-done(((bf16[1,768,256]{2,1,0:T(8,128)(2,1)}), bf16[4,768,256]{2,1,0:T(8,128)(2,1)}) %all-gather.14.cloned.1.call-update) | async-done | bytes 1572880 | tf_op jit(solution)/shard_map/all_gather | solution.py:120
  471.8 4.4 bitcast_convert_fusion
  476.1 27.0 %reduce-scatter.11.cloned.1.call-done = bf16[192,1024]{1,0:T(8,128)(2,1)} async-done(((bf16[768,1024]{1,0:T(8,128)(2,1)}), bf16[192,1024]{1,0:T(8,128)(2,1)}) %reduce-scatter.11.cloned.1.call-update) | async-done | bytes 393232 | tf_op jit(solution)/shard_map/reduce_scatter | solution.py:123
  (91 shorter events, 52.5 us)
Async XLA Ops:
  6.5 465.2 %copy-start = (bf16[1024,1024]{1,0:T(8,128)(2,1)S(1)}, bf16[1024,1024]{1,0:T(8,128)(2,1)}, u32[]{:S(2)}) copy-start(bf16[1024,1024]{1,0:T(8,128)(2,1)} %param.27) | copy-start | bytes 6291460
  6.5 37.1 %all-gather.6.cloned.1.call-start = ((), (), s32[]{:S(2)}) async-start(), calls=%async_computation.4 | async-start | bytes 1310720 | tf_op jit(solution)/shard_map/all_gather | solution.py:43
  17.2 76.7 %reduce-scatter.5.cloned.1.call-start = ((), (), s32[]{:S(2)}) async-start(), calls=%async_computation.5 | async-start | bytes 3932160 | tf_op jit(solution)/shard_map/reduce_scatter | solution.py:115
  56.5 0.7 copy-start.3
  56.5 0.7 copy-start.4
  56.6 89.7 %all-gather.8.cloned.1.call-start = ((), (), s32[]{:S(2)}) async-start(), calls=%async_computation.6 | async-start | bytes 1310720 | tf_op jit(solution)/shard_map/all_gather | solution.py:120
  65.9 6.3 %collective-permute-start = (s32[2,255]{1,0:T(2,128)S(1)}, s32[2,255]{1,0:T(2,128)S(1)}, u32[]{:S(2)}, u32[]{:S(2)}) collective-permute-start(s32[2,255]{1,0:T(2,128)S(1)} %get-tuple-element.19), channel_id=1, source_target_pairs={{0,16},{16,32},{32,48},{48,64},{64,80},{80,96},{96,112},{1,17},{17... | collective-permute-start | bytes 6128 | tf_op jit(solution)/shard_map/ppermute | solution.py:19
  70.7 7.0 %collective-permute-start.1 = (s32[2,255]{1,0:T(2,128)S(1)}, s32[2,255]{1,0:T(2,128)S(1)}, u32[]{:S(2)}, u32[]{:S(2)}) collective-permute-start(s32[2,255]{1,0:T(2,128)S(1)} %get-tuple-element.20), channel_id=1, source_target_pairs={{16,0},{32,16},{48,32},{64,48},{80,64},{96,80},{112,96},{17,1},{33... | collective-permute-start | bytes 6128 | tf_op jit(solution)/shard_map/ppermute | solution.py:21
  96.0 10.8 %collective-permute-start.2 = (bf16[2,255,256]{1,2,0:T(8,128)(2,1)}, bf16[2,255,256]{1,2,0:T(8,128)(2,1)}, u32[]{:S(2)}, u32[]{:S(2)}) collective-permute-start(bf16[2,255,256]{1,2,0:T(8,128)(2,1)} %get-tuple-element.15), channel_id=1, source_target_pairs={{0,16},{16,32},{32,48},{48,64},{64,80},{80,96},{96,112},{1,17},{17... | collective-permute-start | bytes 783368 | tf_op jit(solution)/shard_map/ppermute | solution.py:19
  101.3 13.3 %collective-permute-start.3 = (bf16[2,255,256]{1,2,0:T(8,128)(2,1)}, bf16[2,255,256]{1,2,0:T(8,128)(2,1)}, u32[]{:S(2)}, u32[]{:S(2)}) collective-permute-start(bf16[2,255,256]{1,2,0:T(8,128)(2,1)} %get-tuple-element.16), channel_id=1, source_target_pairs={{16,0},{32,16},{48,32},{64,48},{80,64},{96,80},{112,96},{17,1},{33... | collective-permute-start | bytes 783368 | tf_op jit(solution)/shard_map/ppermute | solution.py:21
  124.8 50.5 %reduce-scatter.7.cloned.1.call-start = ((), (), s32[]{:S(2)}) async-start(), calls=%async_computation.7 | async-start | bytes 1310720 | tf_op jit(solution)/shard_map/reduce_scatter | solution.py:123
  146.3 4.3 copy-start.2
  146.3 29.1 %copy-start.1 = (bf16[128,1024]{1,0:T(8,128)(2,1)S(1)}, bf16[128,1024]{1,0:T(8,128)(2,1)}, u32[]{:S(2)}) copy-start(bf16[128,1024]{1,0:T(8,128)(2,1)} %param.15) | copy-start | bytes 786436
  150.5 72.8 %all-gather.10.cloned.1.call-start = ((), (), s32[]{:S(2)}) async-start(), calls=%async_computation.8 | async-start | bytes 1966080 | tf_op jit(solution)/shard_map/all_gather | solution.py:43
  176.4 8.3 %collective-permute-start.4 = (bf16[128,1024]{1,0:T(8,128)(2,1)S(1)}, bf16[128,1024]{1,0:T(8,128)(2,1)S(1)}, u32[]{:S(2)}, u32[]{:S(2)}) collective-permute-start(bf16[128,1024]{1,0:T(8,128)(2,1)S(1)} %fusion.39), channel_id=1, source_target_pairs={{1,0},{2,1},{3,2},{16,3},{17,16},{18,17},{19,18},{32,19},{33,32},{... | collective-permute-start | bytes 786440 | tf_op jit(solution)/shard_map/ppermute | solution.py:31
  192.6 96.1 %reduce-scatter.9.cloned.1.call-start = ((), (), s32[]{:S(2)}) async-start(), calls=%async_computation.9 | async-start | bytes 5898240 | tf_op jit(solution)/shard_map/reduce_scatter | solution.py:115
  239.1 141.6 %all-gather.12.cloned.1.call-start = ((), (), s32[]{:S(2)}) async-start(), calls=%async_computation.10 | async-start | bytes 7077888 | tf_op jit(solution)/shard_map/all_gather | solution.py:203
  291.1 180.7 %all-gather.14.cloned.1.call-start = ((), (), s32[]{:S(2)}) async-start(), calls=%async_computation.11 | async-start | bytes 1966080 | tf_op jit(solution)/shard_map/all_gather | solution.py:120
  380.7 20.1 %slice-start = ((s8[4718592]{0:T(1024)(128)(4,1)}), s8[4194304]{0:T(1024)(128)(4,1)S(1)}, s32[]{:S(2)}) async-start(s8[4718592]{0:T(1024)(128)(4,1)} %bitcast.96), calls=%async_computation.13 | async-start | bytes 8388608
  386.1 14.7 %slice-start.1 = ((s8[4718592]{0:T(1024)(128)(4,1)}), s8[524288]{0:T(1024)(128)(4,1)S(1)}, s32[]{:S(2)}) async-start(s8[4718592]{0:T(1024)(128)(4,1)} %bitcast.96), calls=%async_computation.14 | async-start | bytes 1048576
  449.0 54.2 %reduce-scatter.11.cloned.1.call-start = ((), (), s32[]{:S(2)}) async-start(), calls=%async_computation.12 | async-start | bytes 1966080 | tf_op jit(solution)/shard_map/reduce_scatter | solution.py:123
Sparse Core Ops, SparseCore 0:
  17.4 26.2 all-gather.5
  56.7 37.1 reduce-scatter.4
  124.9 21.2 all-gather.7
  150.6 24.6 reduce-scatter.6
  192.8 30.5 all-gather.9
  239.2 49.5 reduce-scatter.8
  291.4 89.2 all-gather.11
  449.1 22.6 all-gather.13
  476.3 26.8 reduce-scatter.10
where the time goes:
time: 513 us; the launch traced here: 512 us
  waiting for transfers between devices  283 us (55%)
  other arithmetic  67.9 us (13%)
  matrix products  59.4 us (12%)
  local copies, waits for them, and re-layouts  51.4 us (10%)
  blocking collectives  21.2 us (4%)
  starting transfers between devices  14.6 us (3%)
  between operations  13.5 us (3%)
    all_gather x1, waiting for transfers between devices, per_device(): piece = lax.all_gather(dec_pairs, 'req', axis=1, tiled=True)  83.9 us
    reduce_scatter x2, waiting for transfers between devices, head_project(): return lax.psum_scatter(summed, 'row', scatter_dimension=0, tiled=True)  65.7 us
    reduce_scatter x2, waiting for transfers between devices, out_project_heads(): lax.psum_scatter(summed.astype(jnp.bfloat16), 'col', scatter_dimension=0,...  49.6 us
    all_gather x2, waiting for transfers between devices, out_project_heads(): whole = lax.all_gather(attended, 'row', axis=0, tiled=False)  44.1 us
    sub x1, other arithmetic, attend_block(): weights = jnp.where(allowed[None], jnp.exp(scores - peak), 0.0)  36.8 us
    unnamed x20, local copies, waits for them, and re-layouts  24.3 us
    all_gather x2, waiting for transfers between devices, gather_cols(): return lax.all_gather(values, 'col', axis=0, tiled=True)  20.1 us
    dot_general x2, matrix products, head_project(): jnp.einsum('tf,frc->rtc', values, shaped, preferred_element_type=jnp.floa...  17.3 us
  transfers between devices with their start and end apart: 14, of which 13 were waited for; matrix products, arithmetic and copies ran while one was open for 10% of the time, Pallas kernels for 0%

commit v1 on v0

--- a/solution.py
+++ b/solution.py
@@ -200,7 +200,10 @@
     dec_proj = head_project(dec_cols, (dec_wq, dec_wk, dec_wv))
     dec_rows = dec_cols.shape[0]
     dec_pairs = jnp.stack([dec_proj[:, local : 2 * local], dec_proj[:, 2 * local :]])
-    piece = lax.all_gather(dec_pairs, "req", axis=1, tiled=True)
+    devices = lax.axis_size("req")
+    parts = jnp.stack([dec_pairs for _ in range(devices)])
+    parts = lax.all_to_all(parts, "req", split_axis=0, concat_axis=0)
+    piece = jnp.concatenate(parts, axis=1)
     token_slots = lax.axis_index("req") * dec_rows + jnp.arange(dec_rows, dtype=jnp.int32)
     all_slots = jnp.arange(piece.shape[1], dtype=jnp.int32)
     causal = token_slots[:, None] >= all_slots[None, :]

time: 513 us -> 528 us (1.029)
  local copies, waits for them, and re-layouts: 51.4 us -> 75.2 us
  waiting for transfers between devices: 283 us -> 267 us
  starting transfers between devices: 14.6 us -> 20.9 us
    all_gather x1 -> x0, waiting for transfers between devices: 83.9 us -> none  [per_device(): piece = lax.all_gather(dec_pairs, 'req', axis=1, tiled=True)]
    all_to_all x0 -> x1, waiting for transfers between devices: none -> 68.1 us  [per_device(): parts = lax.all_to_all(parts, 'req', split_axis=0, concat_axis=0)]
    another operation x1 -> x4, local copies, waits for them, and re-layouts: 0.11 us -> 14.9 us  [the longest x2 11.5 us: split_heads(): return values.reshape(values.shape[0], values.shape[1] // HD, HD)]
    slice x2 -> x4, local copies, waits for them, and re-layouts: 6.71 us -> 15.8 us  [per_device(): dec_att = attend_block(dec_proj[:, :local], piece[0], piece[1], causal)]
    all_to_all x0 -> x1, starting transfers between devices: none -> 6.42 us  [per_device(): parts = lax.all_to_all(parts, 'req', split_axis=0, concat_axis=0)]
    unnamed x20 -> x22, local copies, waits for them, and re-layouts: 24.3 us -> 24.3 us
  transfers between devices with their start and end apart: 14 -> 14, of which waited for: 13 -> 13; matrix products, arithmetic and copies ran while one was open for 10% -> 9% of each run, Pallas kernels for 0% -> 0%
where the time goes in v1:
time: 528 us; the launch traced here: 527 us
  waiting for transfers between devices  267 us (51%)
  local copies, waits for them, and re-layouts  75.2 us (14%)
  other arithmetic  67 us (13%)
  matrix products  61.3 us (12%)
  blocking collectives  21.2 us (4%)
  starting transfers between devices  20.9 us (4%)
  between operations  13.8 us (3%)
    all_to_all x1, waiting for transfers between devices, per_device(): parts = lax.all_to_all(parts, 'req', split_axis=0, concat_axis=0)  68.1 us
    reduce_scatter x2, waiting for transfers between devices, head_project(): return lax.psum_scatter(summed, 'row', scatter_dimension=0, tiled=True)  65.8 us
    reduce_scatter x2, waiting for transfers between devices, out_project_heads(): lax.psum_scatter(summed.astype(jnp.bfloat16), 'col', scatter_dimension=0,...  49.6 us
    all_gather x2, waiting for transfers between devices, out_project_heads(): whole = lax.all_gather(attended, 'row', axis=0, tiled=False)  43.6 us
    sub x1, other arithmetic, attend_block(): weights = jnp.where(allowed[None], jnp.exp(scores - peak), 0.0)  36.8 us
    unnamed x22, local copies, waits for them, and re-layouts  24.3 us
    all_gather x2, waiting for transfers between devices, gather_cols(): return lax.all_gather(values, 'col', axis=0, tiled=True)  20.1 us
    dot_general x2, matrix products, head_project(): jnp.einsum('tf,frc->rtc', values, shaped, preferred_element_type=jnp.floa...  17.3 us
  transfers between devices with their start and end apart: 14, of which 13 were waited for; matrix products, arithmetic and copies ran while one was open for 9% of the time, Pallas kernels for 0%

profile of v1, /device:TPU:0, one launch (start us, length us, event | category | flops | bytes accessed | tf_op | source)
XLA Modules:
  0.0 526.7 jit_solution(11769364768176898750)
XLA Ops:
  7.8 7.0 %psum.14 = f32[128]{0:T(128)S(1)} all-reduce(f32[128]{0:T(128)S(1)} %fusion.36), channel_id=1, replica_groups=mesh['req'=8,'row'=4,'col'=4] {'row'}, use_global_device_ids=true, to_apply=%region_3.4 | all-reduce | flops 128 | bytes 1024 | tf_op jit(solution)/shard_map/psum | solution.py:37
  29.2 6.6 %pad_maximum_fusion = bf16[1024,4,3,256]{0,3,2,1:T(8,128)(2,1)} fusion(bf16[1024,4,1,256]{0,3,2,1:T(8,128)(2,1)} %bitcast.95, bf16[1024,4,1,256]{0,3,2,1:T(8,128)(2,1)} %bitcast.94, bf16[1024,4,1,256]{0,3,2,1:T(8,128)(2,1)} %bitcast.93), kind=kLoop, calls=%fused_computation.14 | loop fusion | flops 6291456 | bytes 12582912 | tf_op jit(solution)/shard_map/stack | solution.py:110
  35.7 7.9 %all-gather.5.cloned.1.call-done = bf16[512,1024]{1,0:T(8,128)(2,1)} async-done(((bf16[128,1024]{1,0:T(8,128)(2,1)}), bf16[512,1024]{1,0:T(8,128)(2,1)}) %all-gather.5.cloned.1.call-update) | async-done | bytes 1048592 | tf_op jit(solution)/shard_map/all_gather | solution.py:43
  43.7 8.2 %convolution_convert_fusion.1 = bf16[4,768,512]{1,2,0:T(8,128)(2,1)} fusion(bf16[1024,4,768]{0,2,1:T(8,128)(2,1)} %bitcast.99, bf16[512,1024]{1,0:T(8,128)(2,1)} %all-gather.5.cloned.1.call-done), kind=kOutput, calls=%fused_computation.21 | convolution fusion | flops 3222798336 | bytes 10485760 | tf_op jit(solution)/shard_map/tf,frc->rtc/dot_general | solution.py:113
  51.9 4.7 copy.45
  57.2 8.6 %all_gather.17 = s32[2,512]{1,0:T(2,128)S(1)} all-gather(s32[2,128]{1,0:T(2,128)S(1)} %pad_add_fusion.1), channel_id=1, replica_groups=mesh['req'=8,'row'=4,'col'=4] {'col'}, dimensions={1}, use_global_device_ids=true | all-gather | bytes 5120 | tf_op jit(solution)/shard_map/all_gather | solution.py:149
  65.9 4.9 collective-permute-start
  72.1 5.6 %collective-permute-done.1 = s32[2,255]{1,0:T(2,128)S(1)} collective-permute-done((s32[2,255]{1,0:T(2,128)S(1)}, s32[2,255]{1,0:T(2,128)S(1)}, u32[]{:S(2)}, u32[]{:S(2)}) %collective-permute-start.1) | collective-permute-done | bytes 2072 | tf_op jit(solution)/shard_map/ppermute | solution.py:21
  77.8 16.1 %reduce-scatter.5.cloned.1.call-done = bf16[512,768]{0,1:T(8,128)(2,1)} async-done(((bf16[2048,768]{0,1:T(8,128)(2,1)}), bf16[512,768]{0,1:T(8,128)(2,1)}) %reduce-scatter.5.cloned.1.call-update) | async-done | bytes 786448 | tf_op jit(solution)/shard_map/reduce_scatter | solution.py:115
  96.0 5.3 %collective-permute-start.2 = (bf16[2,255,256]{1,2,0:T(8,128)(2,1)}, bf16[2,255,256]{1,2,0:T(8,128)(2,1)}, u32[]{:S(2)}, u32[]{:S(2)}) collective-permute-start(bf16[2,255,256]{1,2,0:T(8,128)(2,1)} %get-tuple-element.15), channel_id=1, source_target_pairs={{0,16},{16,32},{32,48},{48,64},{64,80},{80,96},{96,112},{1,17},{17... | collective-permute-start | bytes 783368 | tf_op jit(solution)/shard_map/ppermute | solution.py:19
  106.7 7.8 %collective-permute-done.3 = bf16[2,255,256]{1,2,0:T(8,128)(2,1)} collective-permute-done((bf16[2,255,256]{1,2,0:T(8,128)(2,1)}, bf16[2,255,256]{1,2,0:T(8,128)(2,1)}, u32[]{:S(2)}, u32[]{:S(2)}) %collective-permute-start.3) | collective-permute-done | bytes 261152 | tf_op jit(solution)/shard_map/ppermute | solution.py:21
  124.9 21.4 %all-gather.7.cloned.1.call-done = bf16[4,512,256]{2,1,0:T(8,128)(2,1)} async-done(((bf16[1,512,256]{2,1,0:T(8,128)(2,1)}), bf16[4,512,256]{2,1,0:T(8,128)(2,1)}) %all-gather.7.cloned.1.call-update) | async-done | bytes 1048592 | tf_op jit(solution)/shard_map/all_gather | solution.py:120
  152.8 22.6 %reduce-scatter.7.cloned.1.call-done = bf16[128,1024]{1,0:T(8,128)(2,1)} async-done(((bf16[512,1024]{1,0:T(8,128)(2,1)}), bf16[128,1024]{1,0:T(8,128)(2,1)}) %reduce-scatter.7.cloned.1.call-update) | async-done | bytes 262160 | tf_op jit(solution)/shard_map/reduce_scatter | solution.py:123
  179.3 5.5 %collective-permute-done.4 = bf16[128,1024]{1,0:T(8,128)(2,1)} collective-permute-done((bf16[128,1024]{1,0:T(8,128)(2,1)S(1)}, bf16[128,1024]{1,0:T(8,128)(2,1)}, u32[]{:S(2)}, u32[]{:S(2)}) %collective-permute-start.4) | collective-permute-done | bytes 262176 | tf_op jit(solution)/shard_map/ppermute | solution.py:31
  186.3 5.7 %psum.15 = f32[192]{0:T(256)S(1)} all-reduce(f32[192]{0:T(256)S(1)} %get-tuple-element.23), channel_id=1, replica_groups=mesh['req'=8,'row'=4,'col'=4] {'row'}, use_global_device_ids=true, to_apply=%region_9.10 | all-reduce | flops 192 | bytes 1536 | tf_op jit(solution)/shard_map/psum | solution.py:37
  204.8 6.6 %pad_maximum_fusion.1 = bf16[1024,4,3,256]{0,3,2,1:T(8,128)(2,1)} fusion(bf16[1024,4,1,256]{0,3,2,1:T(8,128)(2,1)} %bitcast.98, bf16[1024,4,1,256]{0,3,2,1:T(8,128)(2,1)} %bitcast.97, bf16[1024,4,1,256]{0,3,2,1:T(8,128)(2,1)} %bitcast.96), kind=kLoop, calls=%fused_computation.15 | loop fusion | flops 6291456 | bytes 12582912 | tf_op jit(solution)/shard_map/stack | solution.py:110
  211.5 12.1 %all-gather.9.cloned.1.call-done = bf16[768,1024]{1,0:T(8,128)(2,1)} async-done(((bf16[192,1024]{1,0:T(8,128)(2,1)}), bf16[768,1024]{1,0:T(8,128)(2,1)}) %all-gather.9.cloned.1.call-update) | async-done | bytes 1572880 | tf_op jit(solution)/shard_map/all_gather | solution.py:43
  223.6 9.1 %convolution_convert_fusion = bf16[4,768,768]{1,2,0:T(8,128)(2,1)} fusion(bf16[1024,4,768]{0,2,1:T(8,128)(2,1)} %bitcast.100, bf16[768,1024]{1,0:T(8,128)(2,1)} %all-gather.9.cloned.1.call-done), kind=kOutput, calls=%fused_computation.20 | convolution fusion | flops 4834197504 | bytes 12582912 | tf_op jit(solution)/shard_map/tf,frc->rtc/dot_general | solution.py:113
  232.7 6.6 %copy.53 = bf16[3072,768]{0,1:T(8,128)(2,1)} copy(bf16[3072,768]{1,0:T(8,128)(2,1)} %bitcast.101) | data formatting | bytes 9437184 | tf_op jit(solution)/shard_map/reshape | solution.py:114
  239.4 49.7 %reduce-scatter.9.cloned.1.call-done = bf16[768,768]{0,1:T(8,128)(2,1)} async-done(((bf16[3072,768]{0,1:T(8,128)(2,1)}), bf16[768,768]{0,1:T(8,128)(2,1)}) %reduce-scatter.9.cloned.1.call-update) | async-done | bytes 1179664 | tf_op jit(solution)/shard_map/reduce_scatter | solution.py:115
  294.5 6.4 %all-to-all-start = ((bf16[8,2,768,256]{2,3,1,0:T(8,128)(2,1)}), bf16[8,2,768,256]{2,3,1,0:T(8,128)(2,1)}, u32[]{:S(2)}, u32[]{:S(2)}) async-start(bf16[8,2,768,256]{2,3,1,0:T(8,128)(2,1)} %stack.55), calls=%async_computation.3 | async-start | bytes 12582912 | tf_op jit(solution)/shard_map/all_to_all | solution.py:205
  300.9 5.7 %iota_compare_fusion = pred[768,6144]{1,0:T(8,128)(4,1)} fusion(s32[768]{0:T(1024)S(1)} %iota_add_fusion), kind=kLoop, calls=%fused_computation.12 | loop fusion | flops 4718592 | bytes 4721664 | tf_op jit(solution)/shard_map/ge | solution.py:209
  306.6 68.1 %all-to-all-done = bf16[8,2,768,256]{2,3,1,0:T(8,128)(2,1)} async-done(((bf16[8,2,768,256]{2,3,1,0:T(8,128)(2,1)}), bf16[8,2,768,256]{2,3,1,0:T(8,128)(2,1)}, u32[]{:S(2)}, u32[]{:S(2)}) %all-to-all-start) | async-done | bytes 6291488 | tf_op jit(solution)/shard_map/all_to_all | solution.py:205
  374.7 5.0 fusion.66
  383.1 5.7 %reshape_squeeze.15 = bf16[6144,2,128]{0,2,1:T(8,128)(2,1)} reshape(bf16[1,8,768,256]{2,1,3,0:T(8,128)(2,1)} %copy.55) | data formatting | bytes 6291456 | tf_op jit(solution)/shard_map/reshape;squeeze | solution.py:57
  388.8 5.3 %copy.54 = bf16[1,8,768,256]{2,1,3,0:T(8,128)(2,1)} copy(bf16[1,8,768,256]{2,3,0,1:T(8,128)(2,1)} %get-tuple-element.6) | data formatting | bytes 6291456 | tf_op jit(solution)/shard_map/slice | solution.py:210
  394.1 5.7 %reshape_squeeze.14 = bf16[6144,2,128]{0,2,1:T(8,128)(2,1)} reshape(bf16[1,8,768,256]{2,1,3,0:T(8,128)(2,1)} %copy.54) | data formatting | bytes 6291456 | tf_op jit(solution)/shard_map/reshape;squeeze | solution.py:57
  399.9 16.5 %fusion.74 = f32[2,768,6144]{2,1,0:T(8,128)} fusion(bf16[768,2,128]{0,2,1:T(8,128)(2,1)} %bitcast.105, bf16[6144,2,128]{0,2,1:T(8,128)(2,1)} %reshape_squeeze.15), kind=kOutput, calls=%fused_computation.118 | convolution fusion | flops 2415919104 | bytes 41287680 | tf_op jit(solution)/shard_map/qhd,khd->hqk/dot_general | solution.py:62
  416.3 36.8 %fusion.73 = (f32[2,768]{1,0:T(2,128)S(1)}, bf16[2,768,6144]{2,1,0:T(8,128)(2,1)}) fusion(f32[2,768,6144]{2,1,0:T(8,128)} %fusion.74, pred[768,6144]{1,0:T(8,128)(4,1)S(1)} %bitcast.103), kind=kOutput, calls=%fused_computation.117 | output fusion | flops 75503616 | bytes 61347840 | tf_op jit(solution)/shard_map/sub | solution.py:67
  453.1 10.4 %fusion.32 = bf16[768,2,128]{0,2,1:T(8,128)(2,1)S(1)} fusion(bf16[6144,2,128]{0,2,1:T(8,128)(2,1)} %reshape_squeeze.14, bf16[2,768,6144]{2,1,0:T(8,128)(2,1)} %get-tuple-element.26, f32[768,2]{0,1:T(2,128)S(1)} %bitcast.116), kind=kOutput, calls=%fused_computation.38 | convolution fusion | flops 2416312320 | bytes 22419456 | tf_op jit(solution)/shard_map/hqk,khd->qhd/dot_general | solution.py:69
  464.5 22.1 %all-gather.11.cloned.1.call-done = bf16[4,768,256]{2,1,0:T(8,128)(2,1)} async-done(((bf16[1,768,256]{2,1,0:T(8,128)(2,1)}), bf16[4,768,256]{2,1,0:T(8,128)(2,1)}) %all-gather.11.cloned.1.call-update) | async-done | bytes 1572880 | tf_op jit(solution)/shard_map/all_gather | solution.py:120
  491.1 27.0 %reduce-scatter.11.cloned.1.call-done = bf16[192,1024]{1,0:T(8,128)(2,1)} async-done(((bf16[768,1024]{1,0:T(8,128)(2,1)}), bf16[192,1024]{1,0:T(8,128)(2,1)}) %reduce-scatter.11.cloned.1.call-update) | async-done | bytes 393232 | tf_op jit(solution)/shard_map/reduce_scatter | solution.py:123
  (97 shorter events, 76.2 us)
Async XLA Ops:
  6.5 480.1 %copy-start = (bf16[1024,1024]{1,0:T(8,128)(2,1)S(1)}, bf16[1024,1024]{1,0:T(8,128)(2,1)}, u32[]{:S(2)}) copy-start(bf16[1024,1024]{1,0:T(8,128)(2,1)} %param.27) | copy-start | bytes 6291460
  6.5 37.1 %all-gather.5.cloned.1.call-start = ((), (), s32[]{:S(2)}) async-start(), calls=%async_computation.5 | async-start | bytes 1310720 | tf_op jit(solution)/shard_map/all_gather | solution.py:43
  17.2 76.7 %reduce-scatter.5.cloned.1.call-start = ((), (), s32[]{:S(2)}) async-start(), calls=%async_computation.6 | async-start | bytes 3932160 | tf_op jit(solution)/shard_map/reduce_scatter | solution.py:115
  56.5 0.7 copy-start.4
  56.5 0.7 copy-start.5
  56.6 89.7 %all-gather.7.cloned.1.call-start = ((), (), s32[]{:S(2)}) async-start(), calls=%async_computation.7 | async-start | bytes 1310720 | tf_op jit(solution)/shard_map/all_gather | solution.py:120
  65.9 6.3 %collective-permute-start = (s32[2,255]{1,0:T(2,128)S(1)}, s32[2,255]{1,0:T(2,128)S(1)}, u32[]{:S(2)}, u32[]{:S(2)}) collective-permute-start(s32[2,255]{1,0:T(2,128)S(1)} %get-tuple-element.19), channel_id=1, source_target_pairs={{0,16},{16,32},{32,48},{48,64},{64,80},{80,96},{96,112},{1,17},{17... | collective-permute-start | bytes 6128 | tf_op jit(solution)/shard_map/ppermute | solution.py:19
  70.7 7.0 %collective-permute-start.1 = (s32[2,255]{1,0:T(2,128)S(1)}, s32[2,255]{1,0:T(2,128)S(1)}, u32[]{:S(2)}, u32[]{:S(2)}) collective-permute-start(s32[2,255]{1,0:T(2,128)S(1)} %get-tuple-element.20), channel_id=1, source_target_pairs={{16,0},{32,16},{48,32},{64,48},{80,64},{96,80},{112,96},{17,1},{33... | collective-permute-start | bytes 6128 | tf_op jit(solution)/shard_map/ppermute | solution.py:21
  96.0 10.8 %collective-permute-start.2 = (bf16[2,255,256]{1,2,0:T(8,128)(2,1)}, bf16[2,255,256]{1,2,0:T(8,128)(2,1)}, u32[]{:S(2)}, u32[]{:S(2)}) collective-permute-start(bf16[2,255,256]{1,2,0:T(8,128)(2,1)} %get-tuple-element.15), channel_id=1, source_target_pairs={{0,16},{16,32},{32,48},{48,64},{64,80},{80,96},{96,112},{1,17},{17... | collective-permute-start | bytes 783368 | tf_op jit(solution)/shard_map/ppermute | solution.py:19
  101.3 13.3 %collective-permute-start.3 = (bf16[2,255,256]{1,2,0:T(8,128)(2,1)}, bf16[2,255,256]{1,2,0:T(8,128)(2,1)}, u32[]{:S(2)}, u32[]{:S(2)}) collective-permute-start(bf16[2,255,256]{1,2,0:T(8,128)(2,1)} %get-tuple-element.16), channel_id=1, source_target_pairs={{16,0},{32,16},{48,32},{64,48},{80,64},{96,80},{112,96},{17,1},{33... | collective-permute-start | bytes 783368 | tf_op jit(solution)/shard_map/ppermute | solution.py:21
  124.8 50.5 %reduce-scatter.7.cloned.1.call-start = ((), (), s32[]{:S(2)}) async-start(), calls=%async_computation.8 | async-start | bytes 1310720 | tf_op jit(solution)/shard_map/reduce_scatter | solution.py:123
  146.3 4.3 copy-start.3
  146.3 29.1 %copy-start.1 = (bf16[128,1024]{1,0:T(8,128)(2,1)S(1)}, bf16[128,1024]{1,0:T(8,128)(2,1)}, u32[]{:S(2)}) copy-start(bf16[128,1024]{1,0:T(8,128)(2,1)} %param.15) | copy-start | bytes 786436
  150.5 73.1 %all-gather.9.cloned.1.call-start = ((), (), s32[]{:S(2)}) async-start(), calls=%async_computation.9 | async-start | bytes 1966080 | tf_op jit(solution)/shard_map/all_gather | solution.py:43
  176.4 2.9 copy-start.2
  176.4 8.4 %collective-permute-start.4 = (bf16[128,1024]{1,0:T(8,128)(2,1)S(1)}, bf16[128,1024]{1,0:T(8,128)(2,1)}, u32[]{:S(2)}, u32[]{:S(2)}) collective-permute-start(bf16[128,1024]{1,0:T(8,128)(2,1)S(1)} %fusion.39), channel_id=1, source_target_pairs={{1,0},{2,1},{3,2},{16,3},{17,16},{18,17},{19,18},{32,19},{33,32},{... | collective-permute-start | bytes 786440 | tf_op jit(solution)/shard_map/ppermute | solution.py:31
  192.9 96.1 %reduce-scatter.9.cloned.1.call-start = ((), (), s32[]{:S(2)}) async-start(), calls=%async_computation.10 | async-start | bytes 5898240 | tf_op jit(solution)/shard_map/reduce_scatter | solution.py:115
  294.5 80.2 %all-to-all-start = ((bf16[8,2,768,256]{2,3,1,0:T(8,128)(2,1)}), bf16[8,2,768,256]{2,3,1,0:T(8,128)(2,1)}, u32[]{:S(2)}, u32[]{:S(2)}) async-start(bf16[8,2,768,256]{2,3,1,0:T(8,128)(2,1)} %stack.55), calls=%async_computation.3 | async-start | bytes 12582912 | tf_op jit(solution)/shard_map/all_to_all | solution.py:205
  300.9 185.8 %all-gather.11.cloned.1.call-start = ((), (), s32[]{:S(2)}) async-start(), calls=%async_computation.11 | async-start | bytes 1966080 | tf_op jit(solution)/shard_map/all_gather | solution.py:120
  394.1 22.2 %slice-start = ((s8[4718592]{0:T(1024)(128)(4,1)}), s8[524288]{0:T(1024)(128)(4,1)S(1)}, s32[]{:S(2)}) async-start(s8[4718592]{0:T(1024)(128)(4,1)} %bitcast.102), calls=%async_computation.13 | async-start | bytes 1048576
  399.9 16.5 %slice-start.1 = ((s8[4718592]{0:T(1024)(128)(4,1)}), s8[4194304]{0:T(1024)(128)(4,1)S(1)}, s32[]{:S(2)}) async-start(s8[4718592]{0:T(1024)(128)(4,1)} %bitcast.102), calls=%async_computation.14 | async-start | bytes 8388608
  464.5 53.6 %reduce-scatter.11.cloned.1.call-start = ((), (), s32[]{:S(2)}) async-start(), calls=%async_computation.12 | async-start | bytes 1966080 | tf_op jit(solution)/shard_map/reduce_scatter | solution.py:123
Sparse Core Ops, SparseCore 0:
  17.4 26.2 all-gather.4
  56.7 37.1 reduce-scatter.4
  124.9 21.2 all-gather.6
  150.6 24.6 reduce-scatter.6
  193.0 30.5 all-gather.8
  239.5 49.5 reduce-scatter.8
  464.6 22.0 all-gather.10
  491.2 26.8 reduce-scatter.10
